TPU v7x, 256 devices: a whole 4x4x8 slice. The times are simulated.
256 devices in a mesh: grp: 32 (over y, z_lo, core), tp: 8 (over x, z_hi).
Axes of the slice: x: 4, y: 4, z: 8 (z_hi: 2, z_lo: 4; z = z_hi * 4 + z_lo), core: 2. Of those that a mesh axis runs over, the one named last changes fastest.
Arguments:
- tok_ids: int32 [8192], P('grp'), may hold values from 0 to 16383
- accept: int32 [8192], P('grp'), may hold values 0 or 1
- sub_ids: int32 [8192], P('grp'), may hold values from 0 to 16383
- cache_len: int32 [32], replicated, may hold values from 256 to 3840, as said below
- spill: int32 [32], replicated, may hold values from 0 to 1792, as said below
- embed: bfloat16 [16384, 2048], P('grp', 'tp'), may hold values from -6 to 6
- attn_gain: float32 [2048], replicated, may hold values from 0.25 to 1.75
- w_query: bfloat16 [2048, 2048], P(None, 'tp'), may hold values from -0.125 to 0.125
- w_key: bfloat16 [2048, 512], P(None, 'tp'), as said below
- w_value: bfloat16 [2048, 512], P(None, 'tp'), as said below
- w_out: bfloat16 [2048, 2048], P('tp'), may hold values from -2.5 to 2.5
- mlp_gain: float32 [2048], replicated, may hold values from 0.25 to 1.75
- w_gate: bfloat16 [2048, 5632], P(None, 'tp'), may hold values from -0.125 to 0.125
- w_up: bfloat16 [2048, 5632], P(None, 'tp'), may hold values from -0.125 to 0.125
- w_down: bfloat16 [5632, 2048], P('tp'), may hold values from -0.078125 to 0.078125
- cache_keys: bfloat16 [65536, 512], P('grp', 'tp'), may hold values from -320 to 320, as said below
- cache_values: bfloat16 [65536, 512], P('grp', 'tp'), may hold values from -8 to 8, as said below
Outputs:
- first_out: bfloat16 [8192, 2048], P('grp', 'tp')
- second_out: bfloat16 [8192, 2048], P('grp', 'tp')
Inputs may be any that keep to these rules, and one draw needn't show every extreme that they name: Request g keeps cache_len[g] - spill[g] >= 256 positions in slots from 0 of store g and spill[g] positions in the last slots of store (g xor 1); for every g, cache_len[g] - spill[g] + spill[g xor 1] <= 2048. Of each pair of groups 2k, 2k + 1 at most one has spill above 0. `w_key`: the 2 stored copies of a key-value head are equal. `w_value`: the 2 stored copies of a key-value head are equal. `cache_keys`: the 2 stored copies of a key-value head are equal. `cache_values`: the 2 stored copies of a key-value head are equal.
All inputs are finite; a program needn't handle non-finite values. No bound on the sum of `accept` on one device may be relied on, other than what follows from the above.
Results may differ from a plain program's by a relative error of at most 0.024.
Values may be sent and summed in bfloat16 or wider, within the bound.
No kernel may reach another device: no remote copies, remote signals or barrier semaphores. Data moves between devices by JAX's collectives and lax.ppermute only.
A program may use at most 128 MiB of HBM per device.

v0:
```python
import jax
import jax.numpy as jnp
from jax import lax
from jax.sharding import PartitionSpec as P

HD = 64
EPSILON = 1e-05
SENTINEL = -1e30


def shifted(array, axis, step):
    n = lax.axis_size(axis)
    return lax.ppermute(array, axis, [(i, (i + step) % n) for i in range(n)])


def swapped(array, axis, bit):
    return lax.ppermute(array, axis, [(i, i ^ 1 << bit) for i in range(lax.axis_size(axis))])


def tp_gather(part):
    rows, width = part.shape
    n_x = lax.axis_size("tp") // 2
    me = lax.axis_index("tp")
    mine_x = me // 2
    partner = swapped(part, "tp", 0)
    low_first = me % 2 == 0
    pair = jnp.stack([jnp.where(low_first, part, partner), jnp.where(low_first, partner, part)])
    received = [pair] + [shifted(pair, "tp", 2 * k) for k in range(1, n_x)]
    stacked = jnp.stack(received)
    order = (mine_x - jnp.arange(n_x, dtype=jnp.int32)) % n_x
    full = jnp.take(stacked, order, axis=0)
    return full.transpose(2, 0, 1, 3).reshape(rows, n_x * 2 * width)


def tp_reduce(full):
    rows, total_width = full.shape
    n_x = lax.axis_size("tp") // 2
    me = lax.axis_index("tp")
    mine_x = me // 2
    pieces = full.reshape(rows, n_x, total_width // n_x)
    acc = jnp.take(pieces, mine_x, axis=1).astype(jnp.float32)
    for k in range(1, n_x):
        piece = jnp.take(pieces, (mine_x + k) % n_x, axis=1)
        acc = acc + shifted(piece, "tp", 2 * k).astype(jnp.float32)
    halves = acc.reshape(rows, 2, total_width // n_x // 2)
    low = me % 2 == 0
    mine = jnp.where(low, halves[:, 0], halves[:, 1])
    other = jnp.where(low, halves[:, 1], halves[:, 0])
    got = swapped(other.astype(jnp.bfloat16), "tp", 0)
    return mine + got.astype(jnp.float32)


def rms_normed(values, gain):
    square = jnp.mean(values * values, axis=-1, keepdims=True)
    return (values * lax.rsqrt(square + EPSILON) * gain).astype(jnp.bfloat16)


def rotate(vectors, positions):
    half = vectors.shape[-1] // 2
    exponent = jnp.arange(half, dtype=jnp.float32) * (-2.0 / vectors.shape[-1])
    freqs = jnp.power(jnp.float32(10000.0), exponent)
    angles = positions.astype(jnp.float32)[:, None] * freqs[None, :]
    cosine = jnp.cos(angles)[:, None, :]
    sine = jnp.sin(angles)[:, None, :]
    first = vectors[..., :half]
    second = vectors[..., half:]
    return jnp.concatenate(
        [first * cosine - second * sine, second * cosine + first * sine], axis=-1
    )


def partial_attention(query, keys, values, valid):
    scores = (
        jnp.einsum("pbcgd,pkcd->pbcgk", query, keys, preferred_element_type=jnp.float32) * 0.125
    )
    scores = jnp.where(valid, scores, SENTINEL)
    top = jnp.max(scores, axis=-1)
    weights = jnp.where(valid, jnp.exp(scores - top[..., None]), 0.0)
    total = jnp.sum(weights, axis=-1)
    weighted = jnp.einsum(
        "pbcgk,pkcd->pbcgd",
        weights.astype(jnp.bfloat16),
        values,
        preferred_element_type=jnp.float32,
    )
    return (weighted, top, total)


def on_device(
    tok_ids,
    accept,
    sub_ids,
    cache_len,
    spill,
    embed,
    attn_gain,
    w_query,
    w_key,
    w_value,
    w_out,
    mlp_gain,
    w_gate,
    w_up,
    w_down,
    cache_keys,
    cache_values,
):
    block = tok_ids.shape[0]
    slots = cache_keys.shape[0]
    query_local = w_query.shape[1] // HD
    stored_local = w_key.shape[1] // HD
    per_stored = query_local // stored_local
    group_index = lax.axis_index("grp")
    own_count = cache_len[group_index] - spill[group_index]
    far_count = spill[group_index]
    positions = cache_len[group_index] + jnp.arange(block, dtype=jnp.int32)
    slot_ids = jnp.arange(slots, dtype=jnp.int32)
    tail_ids = slot_ids[block:]
    store_keys = cache_keys.reshape(slots, stored_local, HD)
    store_values = cache_values.reshape(slots, stored_local, HD)
    second_ids = jnp.where(accept == 1, sub_ids, tok_ids)
    table = lax.all_gather(embed, "grp", axis=0, tiled=True)
    both_ids = jnp.concatenate([tok_ids, second_ids])
    x_part = jnp.take(table, both_ids, axis=0)
    rows, width = x_part.shape
    tail_keys, tail_values = swapped((cache_keys[block:], cache_values[block:]), "grp", 0)
    far_keys = tail_keys.reshape(slots - block, stored_local, HD)
    far_values = tail_values.reshape(slots - block, stored_local, HD)
    far_valid = tail_ids >= slots - far_count
    own_valid = slot_ids < own_count
    valid = jnp.concatenate([own_valid, far_valid, jnp.ones((block,), dtype=bool)])
    x_full = tp_gather(x_part)
    normed = rms_normed(x_full.astype(jnp.float32), attn_gain)
    both_positions = jnp.concatenate([positions, positions])
    query = rotate(
        jnp.dot(normed, w_query, preferred_element_type=jnp.float32).reshape(rows, query_local, HD),
        both_positions,
    )
    query = query.astype(jnp.bfloat16).reshape(2, block, stored_local, per_stored, HD)
    new_keys = (
        rotate(
            jnp.dot(normed, w_key, preferred_element_type=jnp.float32).reshape(
                rows, stored_local, HD
            ),
            both_positions,
        )
        .astype(jnp.bfloat16)
        .reshape(2, block, stored_local, HD)
    )
    new_values = (
        jnp.dot(normed, w_value, preferred_element_type=jnp.float32)
        .reshape(2, block, stored_local, HD)
        .astype(jnp.bfloat16)
    )
    cached_keys = jnp.concatenate([store_keys, far_keys], axis=0)
    cached_values = jnp.concatenate([store_values, far_values], axis=0)
    keys = jnp.concatenate(
        [jnp.broadcast_to(cached_keys[None], (2,) + cached_keys.shape), new_keys], axis=1
    )
    values = jnp.concatenate(
        [jnp.broadcast_to(cached_values[None], (2,) + cached_values.shape), new_values], axis=1
    )
    weighted, top, total = partial_attention(query, keys, values, valid)
    attended = weighted / total[..., None]
    mixed = attended.reshape(rows, query_local * HD).astype(jnp.bfloat16)
    head_term = jnp.dot(mixed, w_out, preferred_element_type=jnp.float32)
    head_sum = tp_reduce(head_term.astype(jnp.bfloat16))
    resid_part = (x_part.astype(jnp.float32) + head_sum).astype(jnp.bfloat16)
    resid_full = tp_gather(resid_part)
    normed_mlp = rms_normed(resid_full.astype(jnp.float32), mlp_gain)
    gate = jnp.dot(normed_mlp, w_gate, preferred_element_type=jnp.float32)
    lift = jnp.dot(normed_mlp, w_up, preferred_element_type=jnp.float32)
    hidden = (jax.nn.silu(gate) * lift).astype(jnp.bfloat16)
    down_term = jnp.dot(hidden, w_down, preferred_element_type=jnp.float32)
    down_part = tp_reduce(down_term.astype(jnp.bfloat16))
    out = (resid_part.astype(jnp.float32) + down_part).astype(jnp.bfloat16)
    return (out[:block], out[block:])


def solution(mesh):
    placed = (
        P("grp"),
        P("grp"),
        P("grp"),
        P(),
        P(),
        P("grp", "tp"),
        P(),
        P(None, "tp"),
        P(None, "tp"),
        P(None, "tp"),
        P("tp", None),
        P(),
        P(None, "tp"),
        P(None, "tp"),
        P("tp", None),
        P("grp", "tp"),
        P("grp", "tp"),
    )
    return jax.shard_map(
        on_device,
        mesh=mesh,
        in_specs=placed,
        out_specs=(P("grp", "tp"), P("grp", "tp")),
        check_vma=False,
    )
```

profile of v0, /device:TPU:32, one launch (start us, length us, event | category | flops | bytes accessed | tf_op | source)
XLA Modules:
  0.0 436.3 jit_solution(2578726305064428950)
XLA Ops:
  20.3 61.4 %all-gather.2.cloned.1.call-done = bf16[16384,256]{1,0:T(8,128)(2,1)} async-done(((bf16[512,256]{1,0:T(8,128)(2,1)}), bf16[16384,256]{1,0:T(8,128)(2,1)}) %all-gather.2.cloned.1.call-update) | async-done | bytes 8388624 | tf_op jit(solution)/shard_map/all_gather | solution.py:122
  81.7 6.0 %gather_fusion = bf16[512,256]{1,0:T(8,128)(2,1)S(1)} fusion(bf16[16384,256]{1,0:T(8,128)(2,1)} %all-gather.2.cloned.1.call-done, s32[1024]{0:T(1024)S(1)} %pad_clamp_fusion.1), kind=kCustom, calls=%fused_computation.2 | custom fusion | bytes 526336 | tf_op jit(solution)/shard_map/jit(_take)/gather | solution.py:124
  96.8 10.1 %collective-permute-done.1 = bf16[512,256]{1,0:T(8,128)(2,1)} collective-permute-done((bf16[512,256]{1,0:T(8,128)(2,1)}, bf16[512,256]{1,0:T(8,128)(2,1)}, u32[]{:S(2)}, u32[]{:S(2)}) %collective-permute-start.1) | collective-permute-done | bytes 262176 | tf_op jit(solution)/shard_map/ppermute | solution.py:17
  117.2 7.4 %collective-permute-done.3 = bf16[2,512,256]{2,1,0:T(8,128)(2,1)S(1)} collective-permute-done((bf16[2,512,256]{2,1,0:T(8,128)(2,1)S(1)}, bf16[2,512,256]{2,1,0:T(8,128)(2,1)S(1)}, u32[]{:S(2)}, u32[]{:S(2)}) %collective-permute-start.3) | collective-permute-done | bytes 524320 | tf_op jit(solution)/shard_map/ppermute | solution.py:13
  124.6 9.6 %collective-permute-done.2 = bf16[2,512,256]{2,1,0:T(8,128)(2,1)S(1)} collective-permute-done((bf16[2,512,256]{2,1,0:T(8,128)(2,1)S(1)}, bf16[2,512,256]{2,1,0:T(8,128)(2,1)S(1)}, u32[]{:S(2)}, u32[]{:S(2)}) %collective-permute-start.2) | collective-permute-done | bytes 524320 | tf_op jit(solution)/shard_map/ppermute | solution.py:13
  144.3 5.7 %copy.32 = f32[512,4,2,256]{0,3,2,1:T(8,128)} copy(f32[512,4,2,256]{3,0,2,1:T(8,128)} %convert_bitcast_fusion) | data formatting | bytes 8388608 | tf_op jit(solution)/shard_map/convert_element_type | solution.py:133
  150.1 7.4 %copy.31 = f32[512,4,2,256]{3,2,1,0:T(2,128)} copy(f32[512,4,2,256]{3,0,2,1:T(8,128)} %convert_bitcast_fusion) | data formatting | bytes 8388608 | tf_op jit(solution)/shard_map/convert_element_type | solution.py:133
  170.1 6.4 %reshape.510 = f32[2,256,2048]{2,1,0:T(8,128)} reshape(f32[512,4,2,256]{3,2,1,0:T(2,128)} %copy.31) | data formatting | bytes 8388608 | tf_op jit(solution)/shard_map/convert_element_type | solution.py:133
  179.4 12.5 %bitcast_reduce_fusion = (f32[2,256,4]{1,2,0:T(4,128)S(1)}, f32[2,4096,256,4]{2,1,3,0:T(8,128)}) fusion(pred[4096]{0:T(1024)(128)(4,1)S(1)} %pad_add_fusion, bf16[2,256,4,32]{1,3,2,0:T(8,128)(2,1)S(1)} %get-tuple-element.45, bf16[2,256,4,32]{1,3,2,0:T(8,128)(2,1)S(1)} %get-tuple-element.46, bf16[2,256,1,32]{1,3,0,2:T(8,128)(2,1)S(1)} %get-tuple-element.47, ...), kind=kOutput, calls=%fused_computation.4 | convolution fusion | flops 1102575616 | bytes 34877440 | tf_op jit(solution)/shard_map/pbcgd,pkcd->pbcgk/dot_general | solution.py:74
  191.9 15.6 %fusion.2 = f32[2,256,4]{1,2,0:T(4,128)S(1)} fusion(f32[2,4096,256,4]{2,1,3,0:T(8,128)} %get-tuple-element.44, f32[2,256,4]{1,2,0:T(4,128)S(1)} %get-tuple-element.43, pred[4096]{0:T(1024)(128)(4,1)S(1)} %pad_add_fusion), kind=kLoop, calls=%fused_computation.8 | loop fusion | flops 41940992 | bytes 33574912 | tf_op jit(solution)/shard_map/reduce_sum | solution.py:79
  208.4 15.7 %fusion.33 = bf16[2,256,1,4,64]{1,4,3,0,2:T(8,128)(2,1)S(1)} fusion(f32[2,4096,256,4]{2,1,3,0:T(8,128)} %get-tuple-element.44, f32[2,256,4]{1,2,0:T(4,128)S(1)} %get-tuple-element.43, pred[4096]{0:T(1024)(128)(4,1)S(1)} %pad_add_fusion, bf16[2,256,1,64]{1,3,0,2:T(8,128)(2,1)S(1)} %fusion.26, bf16[2,3840,1,64]{1,3,0,2:T(8,128)(2,1)S(1)} %broadcast_in_dim.78, ...), kind=kOutput, calls=%fused_computation.48 | convolution fusion | flops 1118044160 | bytes 34885632 | tf_op jit(solution)/shard_map/pbcgk,pkcd->pbcgd/dot_general | solution.py:80
  231.1 9.0 %constant_dynamic-slice_fusion.6 = (bf16[512,1,512]{2,1,0:T(2,128)(2,1)}, bf16[512,1,512]{2,1,0:T(2,128)(2,1)S(1)}, bf16[512,1,512]{2,1,0:T(2,128)(2,1)S(1)}, bf16[512,1,512]{2,1,0:T(2,128)(2,1)S(1)}) fusion(bf16[512,4,512]{2,1,0:T(4,128)(2,1)} %reshape.399, s32[]{:T(128)S(6)} %select_n.207, s32[]{:T(128)S(6)} %select_n.211, s32[]{:T(128)S(6)} %select_n.209, ...), kind=kLoop, calls=%fused_computation.136 | loop fusion | bytes 4194320 | tf_op jit(solution)/shard_map/jit(_take) | solution.py:41
  246.2 19.3 %collective-permute-done.8 = bf16[512,512]{1,0:T(8,128)(2,1)} collective-permute-done((bf16[512,512]{1,0:T(8,128)(2,1)S(1)}, bf16[512,512]{1,0:T(8,128)(2,1)}, u32[]{:S(2)}, u32[]{:S(2)}) %collective-permute-start.8) | collective-permute-done | bytes 524320 | tf_op jit(solution)/shard_map/ppermute | solution.py:13
  265.5 4.6 %collective-permute-done.6 = bf16[512,512]{1,0:T(8,128)(2,1)} collective-permute-done((bf16[512,512]{1,0:T(8,128)(2,1)}, bf16[512,512]{1,0:T(8,128)(2,1)}, u32[]{:S(2)}, u32[]{:S(2)}) %collective-permute-start.6) | collective-permute-done | bytes 524320 | tf_op jit(solution)/shard_map/ppermute | solution.py:13
  284.9 11.5 %collective-permute-done.9 = bf16[512,256]{1,0:T(8,128)(2,1)S(1)} collective-permute-done((bf16[512,256]{1,0:T(8,128)(2,1)S(1)}, bf16[512,256]{1,0:T(8,128)(2,1)S(1)}, u32[]{:S(2)}, u32[]{:S(2)}) %collective-permute-start.9) | collective-permute-done | bytes 262176 | tf_op jit(solution)/shard_map/ppermute | solution.py:17
  301.4 9.2 %collective-permute-done.10 = bf16[512,256]{1,0:T(8,128)(2,1)S(1)} collective-permute-done((bf16[512,256]{1,0:T(8,128)(2,1)S(1)}, bf16[512,256]{1,0:T(8,128)(2,1)S(1)}, u32[]{:S(2)}, u32[]{:S(2)}) %collective-permute-start.10) | collective-permute-done | bytes 262176 | tf_op jit(solution)/shard_map/ppermute | solution.py:17
  315.1 12.0 %collective-permute-done.12 = bf16[2,512,256]{2,1,0:T(8,128)(2,1)S(1)} collective-permute-done((bf16[2,512,256]{2,1,0:T(8,128)(2,1)S(1)}, bf16[2,512,256]{2,1,0:T(8,128)(2,1)S(1)}, u32[]{:S(2)}, u32[]{:S(2)}) %collective-permute-start.12) | collective-permute-done | bytes 524320 | tf_op jit(solution)/shard_map/ppermute | solution.py:13
  327.1 10.1 %collective-permute-done.11 = bf16[2,512,256]{2,1,0:T(8,128)(2,1)S(1)} collective-permute-done((bf16[2,512,256]{2,1,0:T(8,128)(2,1)S(1)}, bf16[2,512,256]{2,1,0:T(8,128)(2,1)S(1)}, u32[]{:S(2)}, u32[]{:S(2)}) %collective-permute-start.11) | collective-permute-done | bytes 524320 | tf_op jit(solution)/shard_map/ppermute | solution.py:13
  347.4 5.3 %copy.49 = f32[512,4,2,256]{0,3,2,1:T(8,128)} copy(f32[512,4,2,256]{3,0,2,1:T(8,128)} %convert_bitcast_fusion.1) | data formatting | bytes 8388608 | tf_op jit(solution)/shard_map/convert_element_type | solution.py:170
  359.6 7.6 %convolution_convert_fusion.1 = bf16[512,2048]{1,0:T(8,128)(2,1)} fusion(bf16[704,2048]{1,0:T(8,128)(2,1)S(1)} %copy-done, bf16[2048,704]{0,1:T(8,128)(2,1)} %param.34, bf16[512,2048]{0,1:T(8,128)(2,1)} %copy-done.6, f32[512,704]{0,1:T(8,128)} %fusion.82), kind=kOutput, calls=%fused_computation.31 | convolution fusion | flops 2956001280 | bytes 11403264 | tf_op jit(solution)/shard_map/dot_general | solution.py:174
  371.7 8.1 %constant_dynamic-slice_fusion.1 = (bf16[512,1,512]{2,1,0:T(2,128)(2,1)S(1)}, bf16[512,1,512]{2,1,0:T(2,128)(2,1)S(1)}, bf16[512,1,512]{2,1,0:T(2,128)(2,1)S(1)}, bf16[512,1,512]{2,1,0:T(2,128)(2,1)S(1)}) fusion(bf16[512,4,512]{2,1,0:T(4,128)(2,1)} %reshape.401, s32[]{:T(128)S(6)} %select_n.207, s32[]{:T(128)S(6)} %select_n.211, s32[]{:T(128)S(6)} %select_n.209, ...), kind=kLoop, calls=%fused_computation.131 | loop fusion | bytes 4194320 | tf_op jit(solution)/shard_map/jit(_take) | solution.py:41
  383.1 11.9 %collective-permute-done.16 = bf16[512,512]{1,0:T(8,128)(2,1)S(1)} collective-permute-done((bf16[512,512]{1,0:T(8,128)(2,1)S(1)}, bf16[512,512]{1,0:T(8,128)(2,1)S(1)}, u32[]{:S(2)}, u32[]{:S(2)}) %collective-permute-start.16) | collective-permute-done | bytes 524320 | tf_op jit(solution)/shard_map/ppermute | solution.py:13
  395.0 11.6 %collective-permute-done.14 = bf16[512,512]{1,0:T(8,128)(2,1)S(1)} collective-permute-done((bf16[512,512]{1,0:T(8,128)(2,1)S(1)}, bf16[512,512]{1,0:T(8,128)(2,1)S(1)}, u32[]{:S(2)}, u32[]{:S(2)}) %collective-permute-start.14) | collective-permute-done | bytes 524320 | tf_op jit(solution)/shard_map/ppermute | solution.py:13
  418.1 9.4 %collective-permute-done.17 = bf16[512,256]{1,0:T(8,128)(2,1)S(1)} collective-permute-done((bf16[512,256]{1,0:T(8,128)(2,1)S(1)}, bf16[512,256]{1,0:T(8,128)(2,1)S(1)}, u32[]{:S(2)}, u32[]{:S(2)}) %collective-permute-start.17) | collective-permute-done | bytes 262176 | tf_op jit(solution)/shard_map/ppermute | solution.py:17
  (155 shorter events, 132.1 us)
Async XLA Ops:
  7.2 352.4 %copy-start = (bf16[704,2048]{1,0:T(8,128)(2,1)S(1)}, bf16[704,2048]{1,0:T(8,128)(2,1)}, u32[]{:S(2)}) copy-start(bf16[704,2048]{1,0:T(8,128)(2,1)} %param.35) | copy-start | bytes 8650756
  7.2 85.6 %copy-start.15 = (f32[2048]{0:T(1024)S(1)}, f32[2048]{0:T(1024)}, u32[]{:S(2)}) copy-start(f32[2048]{0:T(1024)} %param.27) | copy-start | bytes 24580
  7.2 74.6 %all-gather.2.cloned.1.call-start = ((), (), s32[]{:S(2)}) async-start(), calls=%async_computation | async-start | bytes 8650752 | tf_op jit(solution)/shard_map/all_gather | solution.py:122
  9.7 106.5 %collective-permute-start = (bf16[1792,64]{0,1:T(8,128)(2,1)}, bf16[1792,64]{0,1:T(8,128)(2,1)}, u32[]{:S(2)}, u32[]{:S(2)}) collective-permute-start(bf16[1792,64]{0,1:T(8,128)(2,1)} %slice.43), channel_id=1, source_target_pairs={{0,8},{8,0},{16,24},{24,16},{32,40},{40,32},{48,56},{56,48},{64,72... | collective-permute-start | bytes 688136 | tf_op jit(solution)/shard_map/ppermute | solution.py:17
  11.3 103.0 %collective-permute-start.5 = (bf16[1792,64]{0,1:T(8,128)(2,1)}, bf16[1792,64]{0,1:T(8,128)(2,1)}, u32[]{:S(2)}, u32[]{:S(2)}) collective-permute-start(bf16[1792,64]{0,1:T(8,128)(2,1)} %slice.45), channel_id=1, source_target_pairs={{0,8},{8,0},{16,24},{24,16},{32,40},{40,32},{48,56},{56,48},{64,72... | collective-permute-start | bytes 688136 | tf_op jit(solution)/shard_map/ppermute | solution.py:17
  18.3 74.5 %copy-start.19 = (pred[512]{0:T(512)(128)(4,1)}, pred[512]{0:T(512)(128)(4,1)S(1)}, u32[]{:S(2)}) copy-start(pred[512]{0:T(512)(128)(4,1)S(1)} %compare_and_fusion.1) | copy-start | bytes 1540
  88.6 18.3 %collective-permute-start.1 = (bf16[512,256]{1,0:T(8,128)(2,1)}, bf16[512,256]{1,0:T(8,128)(2,1)}, u32[]{:S(2)}, u32[]{:S(2)}) collective-permute-start(bf16[512,256]{1,0:T(8,128)(2,1)} %broadcast_select_fusion.2), channel_id=1, source_target_pairs={{0,1},{1,0},{2,3},{3,2},{4,5},{5,4},{6,7},{7,6},{8,9},{9,8},{10,11... | collective-permute-start | bytes 786440 | tf_op jit(solution)/shard_map/ppermute | solution.py:17
  93.4 21.0 %copy-start.9 = (bf16[2048,64]{0,1:T(8,128)(2,1)S(1)}, bf16[2048,64]{0,1:T(8,128)(2,1)}, u32[]{:S(2)}) copy-start(bf16[2048,64]{0,1:T(8,128)(2,1)} %param.36) | copy-start | bytes 786436
  95.8 20.4 %copy-start.10 = (bf16[2048,64]{0,1:T(8,128)(2,1)S(1)}, bf16[2048,64]{0,1:T(8,128)(2,1)}, u32[]{:S(2)}) copy-start(bf16[2048,64]{0,1:T(8,128)(2,1)} %param.37) | copy-start | bytes 786436
  108.1 16.5 %collective-permute-start.3 = (bf16[2,512,256]{2,1,0:T(8,128)(2,1)S(1)}, bf16[2,512,256]{2,1,0:T(8,128)(2,1)S(1)}, u32[]{:S(2)}, u32[]{:S(2)}) collective-permute-start(bf16[2,512,256]{2,1,0:T(8,128)(2,1)S(1)} %get-tuple-element.34), channel_id=1, source_target_pairs={{0,4},{1,5},{2,6},{3,7},{4,0},{5,1},{6,2},{7,3},{8,12},{9,13},{10,... | collective-permute-start | bytes 1572872 | tf_op jit(solution)/shard_map/ppermute | solution.py:13
  111.2 23.0 %collective-permute-start.2 = (bf16[2,512,256]{2,1,0:T(8,128)(2,1)S(1)}, bf16[2,512,256]{2,1,0:T(8,128)(2,1)S(1)}, u32[]{:S(2)}, u32[]{:S(2)}) collective-permute-start(bf16[2,512,256]{2,1,0:T(8,128)(2,1)S(1)} %get-tuple-element.34), channel_id=1, source_target_pairs={{0,2},{1,3},{2,4},{3,5},{4,6},{5,7},{6,0},{7,1},{8,10},{9,11},{10,... | collective-permute-start | bytes 1572872 | tf_op jit(solution)/shard_map/ppermute | solution.py:13
  111.7 22.5 %collective-permute-start.4 = (bf16[2,512,256]{2,1,0:T(8,128)(2,1)S(1)}, bf16[2,512,256]{2,1,0:T(8,128)(2,1)S(1)}, u32[]{:S(2)}, u32[]{:S(2)}) collective-permute-start(bf16[2,512,256]{2,1,0:T(8,128)(2,1)S(1)} %get-tuple-element.34), channel_id=1, source_target_pairs={{0,6},{1,7},{2,0},{3,1},{4,2},{5,3},{6,4},{7,5},{8,14},{9,15},{10,... | collective-permute-start | bytes 1572872 | tf_op jit(solution)/shard_map/ppermute | solution.py:13
  240.2 25.3 %collective-permute-start.8 = (bf16[512,512]{1,0:T(8,128)(2,1)S(1)}, bf16[512,512]{1,0:T(8,128)(2,1)}, u32[]{:S(2)}, u32[]{:S(2)}) collective-permute-start(bf16[512,512]{1,0:T(8,128)(2,1)S(1)} %fusion.47), channel_id=1, source_target_pairs={{0,6},{1,7},{2,0},{3,1},{4,2},{5,3},{6,4},{7,5},{8,14},{9,15},{10,... | collective-permute-start | bytes 1572872 | tf_op jit(solution)/shard_map/ppermute | solution.py:13
  243.8 26.3 %collective-permute-start.6 = (bf16[512,512]{1,0:T(8,128)(2,1)}, bf16[512,512]{1,0:T(8,128)(2,1)}, u32[]{:S(2)}, u32[]{:S(2)}) collective-permute-start(bf16[512,512]{1,0:T(8,128)(2,1)} %fusion.49), channel_id=1, source_target_pairs={{0,2},{1,3},{2,4},{3,5},{4,6},{5,7},{6,0},{7,1},{8,10},{9,11},{10,... | collective-permute-start | bytes 1572872 | tf_op jit(solution)/shard_map/ppermute | solution.py:13
  244.7 25.4 %collective-permute-start.7 = (bf16[512,512]{1,0:T(8,128)(2,1)}, bf16[512,512]{1,0:T(8,128)(2,1)}, u32[]{:S(2)}, u32[]{:S(2)}) collective-permute-start(bf16[512,512]{1,0:T(8,128)(2,1)} %fusion.48), channel_id=1, source_target_pairs={{0,4},{1,5},{2,6},{3,7},{4,0},{5,1},{6,2},{7,3},{8,12},{9,13},{10,... | collective-permute-start | bytes 1572872 | tf_op jit(solution)/shard_map/ppermute | solution.py:13
  282.3 14.1 %collective-permute-start.9 = (bf16[512,256]{1,0:T(8,128)(2,1)S(1)}, bf16[512,256]{1,0:T(8,128)(2,1)S(1)}, u32[]{:S(2)}, u32[]{:S(2)}) collective-permute-start(bf16[512,256]{1,0:T(8,128)(2,1)S(1)} %fusion.55), channel_id=1, source_target_pairs={{0,1},{1,0},{2,3},{3,2},{4,5},{5,4},{6,7},{7,6},{8,9},{9,8},{10,11... | collective-permute-start | bytes 786440 | tf_op jit(solution)/shard_map/ppermute | solution.py:17
  297.6 13.0 %collective-permute-start.10 = (bf16[512,256]{1,0:T(8,128)(2,1)S(1)}, bf16[512,256]{1,0:T(8,128)(2,1)S(1)}, u32[]{:S(2)}, u32[]{:S(2)}) collective-permute-start(bf16[512,256]{1,0:T(8,128)(2,1)S(1)} %fusion.54), channel_id=1, source_target_pairs={{0,1},{1,0},{2,3},{3,2},{4,5},{5,4},{6,7},{7,6},{8,9},{9,8},{10,11... | collective-permute-start | bytes 786440 | tf_op jit(solution)/shard_map/ppermute | solution.py:17
  310.7 16.4 %collective-permute-start.12 = (bf16[2,512,256]{2,1,0:T(8,128)(2,1)S(1)}, bf16[2,512,256]{2,1,0:T(8,128)(2,1)S(1)}, u32[]{:S(2)}, u32[]{:S(2)}) collective-permute-start(bf16[2,512,256]{2,1,0:T(8,128)(2,1)S(1)} %get-tuple-element.30), channel_id=1, source_target_pairs={{0,4},{1,5},{2,6},{3,7},{4,0},{5,1},{6,2},{7,3},{8,12},{9,13},{10,... | collective-permute-start | bytes 1572872 | tf_op jit(solution)/shard_map/ppermute | solution.py:13
  311.7 25.6 %collective-permute-start.11 = (bf16[2,512,256]{2,1,0:T(8,128)(2,1)S(1)}, bf16[2,512,256]{2,1,0:T(8,128)(2,1)S(1)}, u32[]{:S(2)}, u32[]{:S(2)}) collective-permute-start(bf16[2,512,256]{2,1,0:T(8,128)(2,1)S(1)} %get-tuple-element.30), channel_id=1, source_target_pairs={{0,2},{1,3},{2,4},{3,5},{4,6},{5,7},{6,0},{7,1},{8,10},{9,11},{10,... | collective-permute-start | bytes 1572872 | tf_op jit(solution)/shard_map/ppermute | solution.py:13
  311.7 25.6 %collective-permute-start.13 = (bf16[2,512,256]{2,1,0:T(8,128)(2,1)S(1)}, bf16[2,512,256]{2,1,0:T(8,128)(2,1)S(1)}, u32[]{:S(2)}, u32[]{:S(2)}) collective-permute-start(bf16[2,512,256]{2,1,0:T(8,128)(2,1)S(1)} %get-tuple-element.30), channel_id=1, source_target_pairs={{0,6},{1,7},{2,0},{3,1},{4,2},{5,3},{6,4},{7,5},{8,14},{9,15},{10,... | collective-permute-start | bytes 1572872 | tf_op jit(solution)/shard_map/ppermute | solution.py:13
  380.1 14.9 %collective-permute-start.16 = (bf16[512,512]{1,0:T(8,128)(2,1)S(1)}, bf16[512,512]{1,0:T(8,128)(2,1)S(1)}, u32[]{:S(2)}, u32[]{:S(2)}) collective-permute-start(bf16[512,512]{1,0:T(8,128)(2,1)S(1)} %fusion.43), channel_id=1, source_target_pairs={{0,6},{1,7},{2,0},{3,1},{4,2},{5,3},{6,4},{7,5},{8,14},{9,15},{10,... | collective-permute-start | bytes 1572872 | tf_op jit(solution)/shard_map/ppermute | solution.py:13
  380.8 25.8 %collective-permute-start.14 = (bf16[512,512]{1,0:T(8,128)(2,1)S(1)}, bf16[512,512]{1,0:T(8,128)(2,1)S(1)}, u32[]{:S(2)}, u32[]{:S(2)}) collective-permute-start(bf16[512,512]{1,0:T(8,128)(2,1)S(1)} %fusion.45), channel_id=1, source_target_pairs={{0,2},{1,3},{2,4},{3,5},{4,6},{5,7},{6,0},{7,1},{8,10},{9,11},{10,... | collective-permute-start | bytes 1572872 | tf_op jit(solution)/shard_map/ppermute | solution.py:13
  382.2 24.4 %collective-permute-start.15 = (bf16[512,512]{1,0:T(8,128)(2,1)S(1)}, bf16[512,512]{1,0:T(8,128)(2,1)S(1)}, u32[]{:S(2)}, u32[]{:S(2)}) collective-permute-start(bf16[512,512]{1,0:T(8,128)(2,1)S(1)} %fusion.44), channel_id=1, source_target_pairs={{0,4},{1,5},{2,6},{3,7},{4,0},{5,1},{6,2},{7,3},{8,12},{9,13},{10,... | collective-permute-start | bytes 1572872 | tf_op jit(solution)/shard_map/ppermute | solution.py:13
  417.1 10.4 %collective-permute-start.17 = (bf16[512,256]{1,0:T(8,128)(2,1)S(1)}, bf16[512,256]{1,0:T(8,128)(2,1)S(1)}, u32[]{:S(2)}, u32[]{:S(2)}) collective-permute-start(bf16[512,256]{1,0:T(8,128)(2,1)S(1)} %fusion.56), channel_id=1, source_target_pairs={{0,1},{1,0},{2,3},{3,2},{4,5},{5,4},{6,7},{7,6},{8,9},{9,8},{10,11... | collective-permute-start | bytes 786440 | tf_op jit(solution)/shard_map/ppermute | solution.py:17
  (20 other events, 157.2 us)
Sparse Core Ops, SparseCore 0:
  9.9 71.8 all-gather.1
where the time goes:
time: 444 us; the launch traced here: 436 us
  waiting for transfers between devices  189 us (43%)
  local copies, waits for them, and re-layouts  97 us (22%)
  other arithmetic  59.6 us (13%)
  matrix products  44.6 us (10%)
  starting transfers between devices  29.5 us (7%)
  between operations  16.6 us (4%)
    ppermute x12, waiting for transfers between devices, shifted(): return lax.ppermute(array, axis, [(i, (i + step) % n) for i in range(n)])  86.6 us
    all_gather x1, waiting for transfers between devices, on_device(): table = lax.all_gather(embed, 'grp', axis=0, tiled=True)  61.4 us
    ppermute x6, waiting for transfers between devices, swapped(): lax.ppermute(array, axis, [(i, i ^ 1 << bit) for i in range(lax.axis_size...  40.3 us
    convert_element_type x3, local copies, waits for them, and re-layouts, on_device(): normed = rms_normed(x_full.astype(jnp.float32), attn_gain)  19.5 us
    ppermute x12, starting transfers between devices, shifted(): return lax.ppermute(array, axis, [(i, (i + step) % n) for i in range(n)])  17.9 us
    another operation x2, local copies, waits for them, and re-layouts, tp_reduce(): acc = jnp.take(pieces, mine_x, axis=1).astype(jnp.float32)  17.1 us
    dot_general x1, matrix products, partial_attention(): jnp.einsum('pbcgk,pkcd->pbcgd', weights.astype(jnp.bfloat16), values, pre...  15.7 us
    reduce_sum x1, other arithmetic, partial_attention(): total = jnp.sum(weights, axis=-1)  15.6 us
  transfers between devices with their start and end apart: 19, of which 14 were waited for; matrix products, arithmetic and copies ran while one was open for 6% of the time, Pallas kernels for 0%

commit v1 on v0

--- a/solution.py
+++ b/solution.py
@@ -105,6 +105,18 @@
     cache_keys,
     cache_values,
 ):
+
+    def meet_slabs(vals, net_axis, dim_at):
+        return jnp.concatenate(
+            lax.all_to_all(
+                jnp.stack(lax.psum(1, net_axis) * [vals], axis=0),
+                concat_axis=0,
+                split_axis=0,
+                axis_name=net_axis,
+            ),
+            axis=dim_at,
+        )
+
     block = tok_ids.shape[0]
     slots = cache_keys.shape[0]
     query_local = w_query.shape[1] // HD
@@ -119,7 +131,7 @@
     store_keys = cache_keys.reshape(slots, stored_local, HD)
     store_values = cache_values.reshape(slots, stored_local, HD)
     second_ids = jnp.where(accept == 1, sub_ids, tok_ids)
-    table = lax.all_gather(embed, "grp", axis=0, tiled=True)
+    table = meet_slabs(embed, "grp", 0)
     both_ids = jnp.concatenate([tok_ids, second_ids])
     x_part = jnp.take(table, both_ids, axis=0)
     rows, width = x_part.shape

time: 444 us -> 553 us (1.25)
  the two profiles are of different devices: /device:TPU:32 before, /device:TPU:24 now
where the time goes in v1:
time: 553 us; the launch traced here: 545 us
  waiting for transfers between devices  300 us (54%)
  local copies, waits for them, and re-layouts  98.9 us (18%)
  other arithmetic  57.6 us (10%)
  matrix products  44.7 us (8%)
  starting transfers between devices  40.8 us (7%)
    all_to_all x1, waiting for transfers between devices, meet_slabs(): lax.all_to_all(jnp.stack(lax.psum(1, net_axis) * [vals], axis=0), concat_...  176 us
    ppermute x12, waiting for transfers between devices, shifted(): return lax.ppermute(array, axis, [(i, (i + step) % n) for i in range(n)])  85.5 us
    ppermute x6, waiting for transfers between devices, swapped(): lax.ppermute(array, axis, [(i, i ^ 1 << bit) for i in range(lax.axis_size...  37.7 us
    convert_element_type x3, local copies, waits for them, and re-layouts, on_device(): normed = rms_normed(x_full.astype(jnp.float32), attn_gain)  19.6 us
    ppermute x12, starting transfers between devices, shifted(): return lax.ppermute(array, axis, [(i, (i + step) % n) for i in range(n)])  17.9 us
    another operation x2, local copies, waits for them, and re-layouts, tp_reduce(): acc = jnp.take(pieces, mine_x, axis=1).astype(jnp.float32)  17 us
    dot_general x1, matrix products, partial_attention(): jnp.einsum('pbcgk,pkcd->pbcgd', weights.astype(jnp.bfloat16), values, pre...  15.7 us
    reduce_sum x1, other arithmetic, partial_attention(): total = jnp.sum(weights, axis=-1)  15.6 us
  transfers between devices with their start and end apart: 19, of which 14 were waited for; matrix products, arithmetic and copies ran while one was open for 4% of the time, Pallas kernels for 0%

profile of v1, /device:TPU:24, one launch (start us, length us, event | category | flops | bytes accessed | tf_op | source)
XLA Modules:
  0.0 544.9 jit_solution(3738768196180666298)
XLA Ops:
  0.6 5.3 stack.34
  6.0 9.1 %all-to-all-start = ((bf16[32,512,256]{2,1,0:T(8,128)(2,1)}), bf16[32,512,256]{2,1,0:T(8,128)(2,1)}, u32[]{:S(2)}, u32[]{:S(2)}) async-start(bf16[32,512,256]{2,1,0:T(8,128)(2,1)} %stack.34), calls=%async_computation | async-start | bytes 16777216 | tf_op jit(solution)/shard_map/all_to_all | solution.py:111
  22.3 176.4 %all-to-all-done = bf16[32,512,256]{2,1,0:T(8,128)(2,1)} async-done(((bf16[32,512,256]{2,1,0:T(8,128)(2,1)}), bf16[32,512,256]{2,1,0:T(8,128)(2,1)}, u32[]{:S(2)}, u32[]{:S(2)}) %all-to-all-start) | async-done | bytes 8388640 | tf_op jit(solution)/shard_map/all_to_all | solution.py:111
  198.7 6.0 %gather_fusion = bf16[512,256]{1,0:T(8,128)(2,1)S(1)} fusion(bf16[16384,256]{1,0:T(8,128)(2,1)} %bitcast, s32[1024]{0:T(1024)S(1)} %pad_clamp_fusion.1), kind=kCustom, calls=%fused_computation.2 | custom fusion | bytes 526336 | tf_op jit(solution)/shard_map/jit(_take)/gather | solution.py:136
  214.5 9.2 %collective-permute-done.1 = bf16[512,256]{1,0:T(8,128)(2,1)} collective-permute-done((bf16[512,256]{1,0:T(8,128)(2,1)}, bf16[512,256]{1,0:T(8,128)(2,1)}, u32[]{:S(2)}, u32[]{:S(2)}) %collective-permute-start.1) | collective-permute-done | bytes 262176 | tf_op jit(solution)/shard_map/ppermute | solution.py:17
  234.0 7.4 %collective-permute-done.3 = bf16[2,512,256]{2,1,0:T(8,128)(2,1)S(1)} collective-permute-done((bf16[2,512,256]{2,1,0:T(8,128)(2,1)S(1)}, bf16[2,512,256]{2,1,0:T(8,128)(2,1)S(1)}, u32[]{:S(2)}, u32[]{:S(2)}) %collective-permute-start.3) | collective-permute-done | bytes 524320 | tf_op jit(solution)/shard_map/ppermute | solution.py:13
  241.4 9.2 %collective-permute-done.2 = bf16[2,512,256]{2,1,0:T(8,128)(2,1)S(1)} collective-permute-done((bf16[2,512,256]{2,1,0:T(8,128)(2,1)S(1)}, bf16[2,512,256]{2,1,0:T(8,128)(2,1)S(1)}, u32[]{:S(2)}, u32[]{:S(2)}) %collective-permute-start.2) | collective-permute-done | bytes 524320 | tf_op jit(solution)/shard_map/ppermute | solution.py:13
  260.9 5.7 %copy.32 = f32[512,4,2,256]{0,3,2,1:T(8,128)} copy(f32[512,4,2,256]{3,0,2,1:T(8,128)} %convert_bitcast_fusion) | data formatting | bytes 8388608 | tf_op jit(solution)/shard_map/convert_element_type | solution.py:145
  266.7 7.4 %copy.31 = f32[512,4,2,256]{3,2,1,0:T(2,128)} copy(f32[512,4,2,256]{3,0,2,1:T(8,128)} %convert_bitcast_fusion) | data formatting | bytes 8388608 | tf_op jit(solution)/shard_map/convert_element_type | solution.py:145
  286.7 6.4 %reshape.516 = f32[2,256,2048]{2,1,0:T(8,128)} reshape(f32[512,4,2,256]{3,2,1,0:T(2,128)} %copy.31) | data formatting | bytes 8388608 | tf_op jit(solution)/shard_map/convert_element_type | solution.py:145
  296.0 12.6 %bitcast_reduce_fusion = (f32[2,256,4]{1,2,0:T(4,128)S(1)}, f32[2,4096,256,4]{2,1,3,0:T(8,128)}) fusion(pred[4096]{0:T(1024)(128)(4,1)S(1)} %pad_add_fusion, bf16[2,256,4,32]{1,3,2,0:T(8,128)(2,1)S(1)} %get-tuple-element.45, bf16[2,256,4,32]{1,3,2,0:T(8,128)(2,1)S(1)} %get-tuple-element.46, bf16[2,256,1,32]{1,3,0,2:T(8,128)(2,1)S(1)} %get-tuple-element.47, ...), kind=kOutput, calls=%fused_computation.4 | convolution fusion | flops 1102575616 | bytes 34877440 | tf_op jit(solution)/shard_map/pbcgd,pkcd->pbcgk/dot_general | solution.py:74
  308.5 15.6 %fusion.2 = f32[2,256,4]{1,2,0:T(4,128)S(1)} fusion(f32[2,4096,256,4]{2,1,3,0:T(8,128)} %get-tuple-element.44, f32[2,256,4]{1,2,0:T(4,128)S(1)} %get-tuple-element.43, pred[4096]{0:T(1024)(128)(4,1)S(1)} %pad_add_fusion), kind=kLoop, calls=%fused_computation.8 | loop fusion | flops 41940992 | bytes 33574912 | tf_op jit(solution)/shard_map/reduce_sum | solution.py:79
  325.1 15.7 %fusion.33 = bf16[2,256,1,4,64]{1,4,3,0,2:T(8,128)(2,1)S(1)} fusion(f32[2,4096,256,4]{2,1,3,0:T(8,128)} %get-tuple-element.44, f32[2,256,4]{1,2,0:T(4,128)S(1)} %get-tuple-element.43, pred[4096]{0:T(1024)(128)(4,1)S(1)} %pad_add_fusion, bf16[2,256,1,64]{1,3,0,2:T(8,128)(2,1)S(1)} %fusion.26, bf16[2,3840,1,64]{1,3,0,2:T(8,128)(2,1)S(1)} %broadcast_in_dim.78, ...), kind=kOutput, calls=%fused_computation.48 | convolution fusion | flops 1118044160 | bytes 34885632 | tf_op jit(solution)/shard_map/pbcgk,pkcd->pbcgd/dot_general | solution.py:80
  347.7 8.9 %constant_dynamic-slice_fusion.6 = (bf16[512,1,512]{2,1,0:T(2,128)(2,1)}, bf16[512,1,512]{2,1,0:T(2,128)(2,1)S(1)}, bf16[512,1,512]{2,1,0:T(2,128)(2,1)S(1)}, bf16[512,1,512]{2,1,0:T(2,128)(2,1)S(1)}) fusion(bf16[512,4,512]{2,1,0:T(4,128)(2,1)} %reshape.405, s32[]{:T(128)S(6)} %select_n.207, s32[]{:T(128)S(6)} %select_n.211, s32[]{:T(128)S(6)} %select_n.209, ...), kind=kLoop, calls=%fused_computation.136 | loop fusion | bytes 4194320 | tf_op jit(solution)/shard_map/jit(_take) | solution.py:41
  362.7 19.4 %collective-permute-done.8 = bf16[512,512]{1,0:T(8,128)(2,1)} collective-permute-done((bf16[512,512]{1,0:T(8,128)(2,1)S(1)}, bf16[512,512]{1,0:T(8,128)(2,1)}, u32[]{:S(2)}, u32[]{:S(2)}) %collective-permute-start.8) | collective-permute-done | bytes 524320 | tf_op jit(solution)/shard_map/ppermute | solution.py:13
  401.9 11.5 %collective-permute-done.9 = bf16[512,256]{1,0:T(8,128)(2,1)S(1)} collective-permute-done((bf16[512,256]{1,0:T(8,128)(2,1)S(1)}, bf16[512,256]{1,0:T(8,128)(2,1)S(1)}, u32[]{:S(2)}, u32[]{:S(2)}) %collective-permute-start.9) | collective-permute-done | bytes 262176 | tf_op jit(solution)/shard_map/ppermute | solution.py:17
  417.2 9.5 %collective-permute-done.10 = bf16[512,256]{1,0:T(8,128)(2,1)S(1)} collective-permute-done((bf16[512,256]{1,0:T(8,128)(2,1)S(1)}, bf16[512,256]{1,0:T(8,128)(2,1)S(1)}, u32[]{:S(2)}, u32[]{:S(2)}) %collective-permute-start.10) | collective-permute-done | bytes 262176 | tf_op jit(solution)/shard_map/ppermute | solution.py:17
  431.2 12.1 %collective-permute-done.12 = bf16[2,512,256]{2,1,0:T(8,128)(2,1)S(1)} collective-permute-done((bf16[2,512,256]{2,1,0:T(8,128)(2,1)S(1)}, bf16[2,512,256]{2,1,0:T(8,128)(2,1)S(1)}, u32[]{:S(2)}, u32[]{:S(2)}) %collective-permute-start.12) | collective-permute-done | bytes 524320 | tf_op jit(solution)/shard_map/ppermute | solution.py:13
  443.3 9.2 %collective-permute-done.11 = bf16[2,512,256]{2,1,0:T(8,128)(2,1)S(1)} collective-permute-done((bf16[2,512,256]{2,1,0:T(8,128)(2,1)S(1)}, bf16[2,512,256]{2,1,0:T(8,128)(2,1)S(1)}, u32[]{:S(2)}, u32[]{:S(2)}) %collective-permute-start.11) | collective-permute-done | bytes 524320 | tf_op jit(solution)/shard_map/ppermute | solution.py:13
  474.9 7.6 %convolution_convert_fusion.1 = bf16[512,2048]{1,0:T(8,128)(2,1)} fusion(bf16[704,2048]{1,0:T(8,128)(2,1)S(1)} %copy-done, bf16[2048,704]{0,1:T(8,128)(2,1)} %param.34, bf16[512,2048]{0,1:T(8,128)(2,1)} %copy-done.6, f32[512,704]{0,1:T(8,128)} %fusion.82), kind=kOutput, calls=%fused_computation.31 | convolution fusion | flops 2956001280 | bytes 11403264 | tf_op jit(solution)/shard_map/dot_general | solution.py:186
  487.1 8.1 %constant_dynamic-slice_fusion.1 = (bf16[512,1,512]{2,1,0:T(2,128)(2,1)S(1)}, bf16[512,1,512]{2,1,0:T(2,128)(2,1)S(1)}, bf16[512,1,512]{2,1,0:T(2,128)(2,1)S(1)}, bf16[512,1,512]{2,1,0:T(2,128)(2,1)S(1)}) fusion(bf16[512,4,512]{2,1,0:T(4,128)(2,1)} %reshape.407, s32[]{:T(128)S(6)} %select_n.207, s32[]{:T(128)S(6)} %select_n.211, s32[]{:T(128)S(6)} %select_n.209, ...), kind=kLoop, calls=%fused_computation.131 | loop fusion | bytes 4194320 | tf_op jit(solution)/shard_map/jit(_take) | solution.py:41
  498.5 11.9 %collective-permute-done.16 = bf16[512,512]{1,0:T(8,128)(2,1)S(1)} collective-permute-done((bf16[512,512]{1,0:T(8,128)(2,1)S(1)}, bf16[512,512]{1,0:T(8,128)(2,1)S(1)}, u32[]{:S(2)}, u32[]{:S(2)}) %collective-permute-start.16) | collective-permute-done | bytes 524320 | tf_op jit(solution)/shard_map/ppermute | solution.py:13
  510.3 11.6 %collective-permute-done.14 = bf16[512,512]{1,0:T(8,128)(2,1)S(1)} collective-permute-done((bf16[512,512]{1,0:T(8,128)(2,1)S(1)}, bf16[512,512]{1,0:T(8,128)(2,1)S(1)}, u32[]{:S(2)}, u32[]{:S(2)}) %collective-permute-start.14) | collective-permute-done | bytes 524320 | tf_op jit(solution)/shard_map/ppermute | solution.py:13
  535.4 7.5 %collective-permute-done.17 = bf16[512,256]{1,0:T(8,128)(2,1)S(1)} collective-permute-done((bf16[512,256]{1,0:T(8,128)(2,1)S(1)}, bf16[512,256]{1,0:T(8,128)(2,1)S(1)}, u32[]{:S(2)}, u32[]{:S(2)}) %collective-permute-start.17) | collective-permute-done | bytes 262176 | tf_op jit(solution)/shard_map/ppermute | solution.py:17
  (167 shorter events, 138.1 us)
Async XLA Ops:
  0.6 474.3 %copy-start = (bf16[704,2048]{1,0:T(8,128)(2,1)S(1)}, bf16[704,2048]{1,0:T(8,128)(2,1)}, u32[]{:S(2)}) copy-start(bf16[704,2048]{1,0:T(8,128)(2,1)} %param.35) | copy-start | bytes 8650756
  6.0 192.7 %all-to-all-start = ((bf16[32,512,256]{2,1,0:T(8,128)(2,1)}), bf16[32,512,256]{2,1,0:T(8,128)(2,1)}, u32[]{:S(2)}, u32[]{:S(2)}) async-start(bf16[32,512,256]{2,1,0:T(8,128)(2,1)} %stack.34), calls=%async_computation | async-start | bytes 16777216 | tf_op jit(solution)/shard_map/all_to_all | solution.py:111
  15.2 195.4 %copy-start.16 = (f32[2048]{0:T(1024)S(1)}, f32[2048]{0:T(1024)}, u32[]{:S(2)}) copy-start(f32[2048]{0:T(1024)} %param.27) | copy-start | bytes 24580
  15.9 217.1 %collective-permute-start = (bf16[1792,64]{0,1:T(8,128)(2,1)}, bf16[1792,64]{0,1:T(8,128)(2,1)}, u32[]{:S(2)}, u32[]{:S(2)}) collective-permute-start(bf16[1792,64]{0,1:T(8,128)(2,1)} %slice.43), channel_id=1, source_target_pairs={{0,8},{8,0},{16,24},{24,16},{32,40},{40,32},{48,56},{56,48},{64,72... | collective-permute-start | bytes 688136 | tf_op jit(solution)/shard_map/ppermute | solution.py:17
  16.8 214.5 %collective-permute-start.5 = (bf16[1792,64]{0,1:T(8,128)(2,1)}, bf16[1792,64]{0,1:T(8,128)(2,1)}, u32[]{:S(2)}, u32[]{:S(2)}) collective-permute-start(bf16[1792,64]{0,1:T(8,128)(2,1)} %slice.45), channel_id=1, source_target_pairs={{0,8},{8,0},{16,24},{24,16},{32,40},{40,32},{48,56},{56,48},{64,72... | collective-permute-start | bytes 688136 | tf_op jit(solution)/shard_map/ppermute | solution.py:17
  21.0 192.5 %copy-start.21 = (pred[512]{0:T(512)(128)(4,1)}, pred[512]{0:T(512)(128)(4,1)S(1)}, u32[]{:S(2)}) copy-start(pred[512]{0:T(512)(128)(4,1)S(1)} %compare_and_fusion.1) | copy-start | bytes 1540
  204.7 20.2 %copy-start.4 = (bf16[512,256]{1,0:T(8,128)(2,1)}, bf16[512,256]{1,0:T(8,128)(2,1)S(1)}, u32[]{:S(2)}) copy-start(bf16[512,256]{1,0:T(8,128)(2,1)S(1)} %gather_fusion) | copy-start | bytes 786436
  205.6 18.1 %collective-permute-start.1 = (bf16[512,256]{1,0:T(8,128)(2,1)}, bf16[512,256]{1,0:T(8,128)(2,1)}, u32[]{:S(2)}, u32[]{:S(2)}) collective-permute-start(bf16[512,256]{1,0:T(8,128)(2,1)} %broadcast_select_fusion.2), channel_id=1, source_target_pairs={{0,1},{1,0},{2,3},{3,2},{4,5},{5,4},{6,7},{7,6},{8,9},{9,8},{10,11... | collective-permute-start | bytes 786440 | tf_op jit(solution)/shard_map/ppermute | solution.py:17
  213.5 19.6 %copy-start.11 = (bf16[2048,64]{0,1:T(8,128)(2,1)S(1)}, bf16[2048,64]{0,1:T(8,128)(2,1)}, u32[]{:S(2)}) copy-start(bf16[2048,64]{0,1:T(8,128)(2,1)} %param.37) | copy-start | bytes 786436
  224.9 16.5 %collective-permute-start.3 = (bf16[2,512,256]{2,1,0:T(8,128)(2,1)S(1)}, bf16[2,512,256]{2,1,0:T(8,128)(2,1)S(1)}, u32[]{:S(2)}, u32[]{:S(2)}) collective-permute-start(bf16[2,512,256]{2,1,0:T(8,128)(2,1)S(1)} %get-tuple-element.34), channel_id=1, source_target_pairs={{0,4},{1,5},{2,6},{3,7},{4,0},{5,1},{6,2},{7,3},{8,12},{9,13},{10,... | collective-permute-start | bytes 1572872 | tf_op jit(solution)/shard_map/ppermute | solution.py:13
  228.0 22.6 %collective-permute-start.2 = (bf16[2,512,256]{2,1,0:T(8,128)(2,1)S(1)}, bf16[2,512,256]{2,1,0:T(8,128)(2,1)S(1)}, u32[]{:S(2)}, u32[]{:S(2)}) collective-permute-start(bf16[2,512,256]{2,1,0:T(8,128)(2,1)S(1)} %get-tuple-element.34), channel_id=1, source_target_pairs={{0,2},{1,3},{2,4},{3,5},{4,6},{5,7},{6,0},{7,1},{8,10},{9,11},{10,... | collective-permute-start | bytes 1572872 | tf_op jit(solution)/shard_map/ppermute | solution.py:13
  228.6 22.1 %collective-permute-start.4 = (bf16[2,512,256]{2,1,0:T(8,128)(2,1)S(1)}, bf16[2,512,256]{2,1,0:T(8,128)(2,1)S(1)}, u32[]{:S(2)}, u32[]{:S(2)}) collective-permute-start(bf16[2,512,256]{2,1,0:T(8,128)(2,1)S(1)} %get-tuple-element.34), channel_id=1, source_target_pairs={{0,6},{1,7},{2,0},{3,1},{4,2},{5,3},{6,4},{7,5},{8,14},{9,15},{10,... | collective-permute-start | bytes 1572872 | tf_op jit(solution)/shard_map/ppermute | solution.py:13
  356.7 25.3 %collective-permute-start.8 = (bf16[512,512]{1,0:T(8,128)(2,1)S(1)}, bf16[512,512]{1,0:T(8,128)(2,1)}, u32[]{:S(2)}, u32[]{:S(2)}) collective-permute-start(bf16[512,512]{1,0:T(8,128)(2,1)S(1)} %fusion.47), channel_id=1, source_target_pairs={{0,6},{1,7},{2,0},{3,1},{4,2},{5,3},{6,4},{7,5},{8,14},{9,15},{10,... | collective-permute-start | bytes 1572872 | tf_op jit(solution)/shard_map/ppermute | solution.py:13
  360.3 26.3 %collective-permute-start.6 = (bf16[512,512]{1,0:T(8,128)(2,1)}, bf16[512,512]{1,0:T(8,128)(2,1)}, u32[]{:S(2)}, u32[]{:S(2)}) collective-permute-start(bf16[512,512]{1,0:T(8,128)(2,1)} %fusion.49), channel_id=1, source_target_pairs={{0,2},{1,3},{2,4},{3,5},{4,6},{5,7},{6,0},{7,1},{8,10},{9,11},{10,... | collective-permute-start | bytes 1572872 | tf_op jit(solution)/shard_map/ppermute | solution.py:13
  361.2 25.4 %collective-permute-start.7 = (bf16[512,512]{1,0:T(8,128)(2,1)}, bf16[512,512]{1,0:T(8,128)(2,1)}, u32[]{:S(2)}, u32[]{:S(2)}) collective-permute-start(bf16[512,512]{1,0:T(8,128)(2,1)} %fusion.48), channel_id=1, source_target_pairs={{0,4},{1,5},{2,6},{3,7},{4,0},{5,1},{6,2},{7,3},{8,12},{9,13},{10,... | collective-permute-start | bytes 1572872 | tf_op jit(solution)/shard_map/ppermute | solution.py:13
  398.8 14.6 %collective-permute-start.9 = (bf16[512,256]{1,0:T(8,128)(2,1)S(1)}, bf16[512,256]{1,0:T(8,128)(2,1)S(1)}, u32[]{:S(2)}, u32[]{:S(2)}) collective-permute-start(bf16[512,256]{1,0:T(8,128)(2,1)S(1)} %fusion.55), channel_id=1, source_target_pairs={{0,1},{1,0},{2,3},{3,2},{4,5},{5,4},{6,7},{7,6},{8,9},{9,8},{10,11... | collective-permute-start | bytes 786440 | tf_op jit(solution)/shard_map/ppermute | solution.py:17
  414.6 12.1 %collective-permute-start.10 = (bf16[512,256]{1,0:T(8,128)(2,1)S(1)}, bf16[512,256]{1,0:T(8,128)(2,1)S(1)}, u32[]{:S(2)}, u32[]{:S(2)}) collective-permute-start(bf16[512,256]{1,0:T(8,128)(2,1)S(1)} %fusion.54), channel_id=1, source_target_pairs={{0,1},{1,0},{2,3},{3,2},{4,5},{5,4},{6,7},{7,6},{8,9},{9,8},{10,11... | collective-permute-start | bytes 786440 | tf_op jit(solution)/shard_map/ppermute | solution.py:17
  426.8 16.5 %collective-permute-start.12 = (bf16[2,512,256]{2,1,0:T(8,128)(2,1)S(1)}, bf16[2,512,256]{2,1,0:T(8,128)(2,1)S(1)}, u32[]{:S(2)}, u32[]{:S(2)}) collective-permute-start(bf16[2,512,256]{2,1,0:T(8,128)(2,1)S(1)} %get-tuple-element.30), channel_id=1, source_target_pairs={{0,4},{1,5},{2,6},{3,7},{4,0},{5,1},{6,2},{7,3},{8,12},{9,13},{10,... | collective-permute-start | bytes 1572872 | tf_op jit(solution)/shard_map/ppermute | solution.py:13
  427.8 24.7 %collective-permute-start.11 = (bf16[2,512,256]{2,1,0:T(8,128)(2,1)S(1)}, bf16[2,512,256]{2,1,0:T(8,128)(2,1)S(1)}, u32[]{:S(2)}, u32[]{:S(2)}) collective-permute-start(bf16[2,512,256]{2,1,0:T(8,128)(2,1)S(1)} %get-tuple-element.30), channel_id=1, source_target_pairs={{0,2},{1,3},{2,4},{3,5},{4,6},{5,7},{6,0},{7,1},{8,10},{9,11},{10,... | collective-permute-start | bytes 1572872 | tf_op jit(solution)/shard_map/ppermute | solution.py:13
  427.8 24.7 %collective-permute-start.13 = (bf16[2,512,256]{2,1,0:T(8,128)(2,1)S(1)}, bf16[2,512,256]{2,1,0:T(8,128)(2,1)S(1)}, u32[]{:S(2)}, u32[]{:S(2)}) collective-permute-start(bf16[2,512,256]{2,1,0:T(8,128)(2,1)S(1)} %get-tuple-element.30), channel_id=1, source_target_pairs={{0,6},{1,7},{2,0},{3,1},{4,2},{5,3},{6,4},{7,5},{8,14},{9,15},{10,... | collective-permute-start | bytes 1572872 | tf_op jit(solution)/shard_map/ppermute | solution.py:13
  495.5 14.9 %collective-permute-start.16 = (bf16[512,512]{1,0:T(8,128)(2,1)S(1)}, bf16[512,512]{1,0:T(8,128)(2,1)S(1)}, u32[]{:S(2)}, u32[]{:S(2)}) collective-permute-start(bf16[512,512]{1,0:T(8,128)(2,1)S(1)} %fusion.43), channel_id=1, source_target_pairs={{0,6},{1,7},{2,0},{3,1},{4,2},{5,3},{6,4},{7,5},{8,14},{9,15},{10,... | collective-permute-start | bytes 1572872 | tf_op jit(solution)/shard_map/ppermute | solution.py:13
  496.2 25.8 %collective-permute-start.14 = (bf16[512,512]{1,0:T(8,128)(2,1)S(1)}, bf16[512,512]{1,0:T(8,128)(2,1)S(1)}, u32[]{:S(2)}, u32[]{:S(2)}) collective-permute-start(bf16[512,512]{1,0:T(8,128)(2,1)S(1)} %fusion.45), channel_id=1, source_target_pairs={{0,2},{1,3},{2,4},{3,5},{4,6},{5,7},{6,0},{7,1},{8,10},{9,11},{10,... | collective-permute-start | bytes 1572872 | tf_op jit(solution)/shard_map/ppermute | solution.py:13
  497.6 24.4 %collective-permute-start.15 = (bf16[512,512]{1,0:T(8,128)(2,1)S(1)}, bf16[512,512]{1,0:T(8,128)(2,1)S(1)}, u32[]{:S(2)}, u32[]{:S(2)}) collective-permute-start(bf16[512,512]{1,0:T(8,128)(2,1)S(1)} %fusion.44), channel_id=1, source_target_pairs={{0,4},{1,5},{2,6},{3,7},{4,0},{5,1},{6,2},{7,3},{8,12},{9,13},{10,... | collective-permute-start | bytes 1572872 | tf_op jit(solution)/shard_map/ppermute | solution.py:13
  532.4 10.4 %collective-permute-start.17 = (bf16[512,256]{1,0:T(8,128)(2,1)S(1)}, bf16[512,256]{1,0:T(8,128)(2,1)S(1)}, u32[]{:S(2)}, u32[]{:S(2)}) collective-permute-start(bf16[512,256]{1,0:T(8,128)(2,1)S(1)} %fusion.56), channel_id=1, source_target_pairs={{0,1},{1,0},{2,3},{3,2},{4,5},{5,4},{6,7},{7,6},{8,9},{9,8},{10,11... | collective-permute-start | bytes 786440 | tf_op jit(solution)/shard_map/ppermute | solution.py:17
  (26 other events, 223.6 us)
